TPU v7x, 512 devices: a whole 4x8x8 slice. The times are simulated.
512 devices in a mesh: dp: 64 (over z, x, core), mp: 8 (over y).
Axes of the slice: x: 4, y: 8, z: 8, core: 2. Of those that a mesh axis runs over, the one named last changes fastest.
Arguments:
- micro_grads: bfloat16 [64, 2, 768, 768], P('dp', None, None, 'mp'), may hold values from -16 to 16
- master: float32 [768, 768], P('dp', 'mp'), may hold values from -0.21875 to 0.21875
- moment: float32 [768, 768], P('dp', 'mp'), may hold values from -1.5 to 1.5
- second: float32 [768, 768], P('dp', 'mp'), may hold values from 0.001 to 0.1
- left_basis: float32 [768, 768], P(None, 'dp'), may hold values from -0.21875 to 0.21875
- right_basis: float32 [768, 768], P(None, 'mp'), may hold values from -0.21875 to 0.21875
- left_stat: float32 [768, 768], P('mp'), may hold values from -2 to 5, as said below
- right_stat: float32 [768, 768], P('mp'), may hold values from -2 to 5, as said below
Outputs:
- weights_block: bfloat16 [768, 768], P(None, 'mp')
- new_master: float32 [768, 768], P('dp', 'mp')
- new_moment: float32 [768, 768], P('dp', 'mp')
- new_second: float32 [768, 768], P('dp', 'mp')
- new_left_stat: float32 [768, 768], P('mp')
- new_right_stat: float32 [768, 768], P('mp')
- new_left_basis: float32 [768, 768], P('mp')
- new_right_basis: float32 [768, 768], P('mp')
Inputs may be any that keep to these rules, and one draw needn't show every extreme that they name: `left_stat`: symmetric. `right_stat`: symmetric.
All inputs are finite; a program needn't handle non-finite values.
Results may differ from a plain program's by a relative error of at most 0.004.
The roundings to bfloat16 on the way count: a program that leaves them out, or rounds other values in their place, can miss the bound.
Values may be sent and summed in bfloat16 or wider, within the bound.
No kernel may reach another device: no remote copies, remote signals or barrier semaphores. Data moves between devices by JAX's collectives and lax.ppermute only.
A program may use at most 64 MiB of HBM per device.

v0:
```python
import jax
import jax.numpy as jnp
from jax import lax
from jax.sharding import PartitionSpec as P

beta_one = 0.9
beta_two = 0.95
beta_stat = 0.95
learn_rate = 0.02
adam_eps = 1e-08
norm_eps = 1e-06
quint_a = 1.875
quint_b = -1.25
quint_c = 0.375
highest = lax.Precision.HIGHEST


def for_sending(x):

    def short(part):
        return part.astype(jnp.bfloat16) if part.dtype == jnp.float32 else part

    return jax.tree.map(short, x)


def all_rows(pair):
    return jax.tree.map(
        lambda part, own: part.astype(own.dtype),
        lax.all_gather(for_sending(pair), "mp", axis=0, tiled=True),
        pair,
    )


def row_gram(row_part, whole_part):
    return lax.dot_general(
        row_part, whole_part, (((1,), (1,)), ((), ())), preferred_element_type=jnp.float32
    )


def scatter_sum(x, axis):
    count = lax.axis_size(axis)
    chunks = x.reshape((count, x.shape[0] // count) + x.shape[1:])
    return jnp.sum(lax.all_to_all(chunks, axis, 0, 0, tiled=False), axis=0)


def gather_rows(x, axis):
    count = lax.axis_size(axis)
    return lax.all_to_all(jnp.broadcast_to(x[None], (count,) + x.shape), axis, 0, 0, tiled=False)


def per_device(micro_grads, master, moment, second, left_basis, right_basis, left_stat, right_stat):
    dp_count = lax.axis_size("dp")
    micro_count = micro_grads.shape[1]
    local_sum = jnp.sum(micro_grads[0], axis=0, dtype=jnp.float32)
    grad_piece = scatter_sum(local_sum, "dp") / (micro_count * dp_count)
    new_moment = beta_one * moment + (1.0 - beta_one) * grad_piece
    pieces = gather_rows(jnp.stack([grad_piece, new_moment]), "dp")
    pieces = jnp.swapaxes(pieces, 0, 1).reshape(2, -1, pieces.shape[-1])
    left_full = lax.all_gather(left_basis, "dp", axis=1, tiled=True)
    both_full = lax.all_gather(pieces, "mp", axis=2, tiled=True)
    right_full = lax.all_gather(right_basis, "mp", axis=1, tiled=True)
    grad_full = both_full[0]
    moment_full = both_full[1]

    def rotate(matrix):
        left_part = lax.dot_general(left_basis, matrix, (((0,), (0,)), ((), ())), precision=highest)
        return jnp.dot(left_part, right_basis, precision=highest)

    rot_grad = rotate(grad_full)
    rot_moment = rotate(moment_full)
    new_second = beta_two * second + (1.0 - beta_two) * rot_grad * rot_grad
    rot_step = rot_moment / (jnp.sqrt(new_second) + adam_eps)
    back_half = scatter_sum(
        lax.dot_general(right_basis, rot_step, (((1,), (1,)), ((), ())), precision=highest), "mp"
    )
    step_piece = scatter_sum(
        lax.dot_general(left_basis, back_half, (((1,), (1,)), ((), ())), precision=highest), "dp"
    )
    new_master = master - learn_rate * step_piece
    weights_block = gather_rows(new_master.astype(jnp.bfloat16), "dp").reshape(
        -1, new_master.shape[1]
    )
    band_width = right_basis.shape[1]
    band_start = lax.axis_index("mp") * band_width
    grad_band = lax.dynamic_slice_in_dim(grad_full, band_start, band_width, 0)
    grad_strip = lax.dynamic_slice_in_dim(grad_full, band_start, band_width, 1)
    left_outer = lax.dot_general(grad_band, grad_full, (((1,), (1,)), ((), ())), precision=highest)
    right_outer = lax.dot_general(
        grad_strip, grad_full, (((0,), (0,)), ((), ())), precision=highest
    )
    new_left_stat = beta_stat * left_stat + (1.0 - beta_stat) * left_outer
    new_right_stat = beta_stat * right_stat + (1.0 - beta_stat) * right_outer
    order_count = left_stat.shape[1]
    power_left = jnp.dot(
        new_left_stat.astype(jnp.bfloat16),
        left_full.astype(jnp.bfloat16),
        preferred_element_type=jnp.float32,
    )
    power_right = jnp.dot(
        new_right_stat.astype(jnp.bfloat16),
        right_full.astype(jnp.bfloat16),
        preferred_element_type=jnp.float32,
    )
    total_left, total_right = lax.psum(
        (jnp.sum(power_left * power_left), jnp.sum(power_right * power_right)), "mp"
    )
    start_left = lax.optimization_barrier(
        (power_left * lax.rsqrt(total_left * (4.0 / order_count) + norm_eps)).astype(jnp.bfloat16)
    )
    start_right = lax.optimization_barrier(
        (power_right * lax.rsqrt(total_right * (4.0 / order_count) + norm_eps)).astype(jnp.bfloat16)
    )
    start_rows = (start_left, start_right)
    start_whole = all_rows(start_rows)
    gram_rows = tuple(
        (
            lax.optimization_barrier(row_gram(row_part, whole_part).astype(jnp.bfloat16))
            for row_part, whole_part in zip(start_rows, start_whole)
        )
    )
    gram_whole = all_rows(gram_rows)
    middle_rows = []
    for row_part, gram_part, gram_all, whole_part in zip(
        start_rows, gram_rows, gram_whole, start_whole
    ):
        square = jnp.dot(gram_part, gram_all, preferred_element_type=jnp.float32)
        poly_rows = (quint_b * gram_part.astype(jnp.float32) + quint_c * square).astype(
            jnp.bfloat16
        )
        middle = quint_a * row_part.astype(jnp.float32) + jnp.dot(
            poly_rows, whole_part, preferred_element_type=jnp.float32
        )
        middle_rows.append(lax.optimization_barrier(middle.astype(jnp.bfloat16)))
    middle_whole = all_rows(tuple(middle_rows))
    new_bases = []
    for row_part, whole_part in zip(middle_rows, middle_whole):
        gram_two = row_gram(row_part, whole_part).astype(jnp.bfloat16)
        new_bases.append(
            1.5 * row_part.astype(jnp.float32)
            - 0.5 * jnp.dot(gram_two, whole_part, preferred_element_type=jnp.float32)
        )
    return (
        weights_block,
        new_master,
        new_moment,
        new_second,
        new_left_stat,
        new_right_stat,
        new_bases[0],
        new_bases[1],
    )


def solution(mesh):
    in_specs = (
        P("dp", None, None, "mp"),
        P("dp", "mp"),
        P("dp", "mp"),
        P("dp", "mp"),
        P(None, "dp"),
        P(None, "mp"),
        P("mp", None),
        P("mp", None),
    )
    out_specs = (
        P(None, "mp"),
        P("dp", "mp"),
        P("dp", "mp"),
        P("dp", "mp"),
        P("mp", None),
        P("mp", None),
        P("mp", None),
        P("mp", None),
    )
    return jax.shard_map(
        per_device, mesh=mesh, in_specs=in_specs, out_specs=out_specs, check_vma=False
    )
```

profile of v0, /device:TPU:2, one launch (start us, length us, event | category | flops | bytes accessed | tf_op | source)
XLA Modules:
  0.0 490.6 jit_solution(16406727266121706216)
XLA Ops:
  7.2 1.4 bitcast_convert_fusion
  8.7 1.0 convert_reduce_fusion
  10.0 31.4 %all_to_all.25 = f32[64,12,96]{2,1,0:T(8,128)S(1)} all-to-all(f32[64,12,96]{2,1,0:T(8,128)S(1)} %reshape.45), channel_id=1, replica_groups=mesh['dp'=64,'mp'=8] {'dp'}, dimensions={0} | all-to-all | bytes 589824 | tf_op jit(solution)/shard_map/all_to_all | solution.py:43
  41.7 28.9 %all_to_all.26 = f32[64,2,12,96]{3,1,2,0:T(2,128)S(1)} all-to-all(f32[64,2,12,96]{3,1,2,0:T(2,128)S(1)} %broadcast_in_dim.4), channel_id=1, replica_groups=mesh['dp'=64,'mp'=8] {'dp'}, dimensions={0} | all-to-all | bytes 1179648 | tf_op jit(solution)/shard_map/all_to_all | solution.py:48
  70.6 1.2 copy.22
  72.7 27.0 %all-gather.27.cloned.1.call-done = bf16[64,12,768]{2,1,0:T(8,128)(2,1)} async-done(((bf16[1,12,768]{2,1,0:T(8,128)(2,1)}), bf16[64,12,768]{2,1,0:T(8,128)(2,1)}) %all-gather.27.cloned.1.call-update) | async-done | bytes 1179664 | tf_op jit(solution)/shard_map/all_gather | solution.py:59
  99.7 3.1 reshape.52
  102.9 59.1 %all-gather.11.cloned.1.call-done = f32[2,768,768]{1,0,2:T(2,128)} async-done(((f32[2,768,96]{1,0,2:T(2,128)}), f32[2,768,768]{1,0,2:T(2,128)}) %all-gather.11.cloned.1.call-update) | async-done | bytes 4718608 | tf_op jit(solution)/shard_map/all_gather | solution.py:60
  162.0 9.3 %fusion.53 = (f32[1,768,768]{1,0,2:T(1,128)S(1)}, f32[1,768,768]{1,0,2:T(1,128)}) fusion(f32[2,768,768]{1,0,2:T(2,128)} %all-gather.11.cloned.1.call-done), kind=kLoop, calls=%fused_computation.70 | loop fusion | bytes 9437184 | tf_op jit(solution)/shard_map/slice | solution.py:62
  171.4 0.9 constant_dynamic-slice_fusion.1
  172.3 1.5 fusion.23
  173.8 1.8 multiply_reduce_fusion.1
  175.7 2.4 fusion.20
  178.1 27.0 %all-gather.19.cloned.1.call-done = bf16[768,768]{0,1:T(8,128)(2,1)} async-done(((bf16[768,96]{0,1:T(8,128)(2,1)}), bf16[768,768]{0,1:T(8,128)(2,1)}) %all-gather.19.cloned.1.call-update) | async-done | bytes 1179664 | tf_op jit(solution)/shard_map/all_gather | solution.py:61
  205.1 2.4 multiply_reduce_fusion
  207.5 16.5 %all-reduce = (f32[]{:T(128)}, f32[]{:T(128)}) all-reduce(f32[]{:T(128)} %get-tuple-element.32, f32[]{:T(128)} %get-tuple-element.34), channel_id=1, replica_groups=mesh['dp'=64,'mp'=8] {'mp'}, use_global_device_ids=true, to_apply=%region_5.0 | all-reduce | flops 2 | bytes 16 | tf_op jit(solution)/shard_map/psum | solution.py:104
  227.0 39.7 %all-gather.21.cloned.1.call-done = bf16[768,768]{1,0:T(8,128)(2,1)} async-done(((bf16[96,768]{1,0:T(8,128)(2,1)}), bf16[768,768]{1,0:T(8,128)(2,1)}) %all-gather.21.cloned.1.call-update) | async-done | bytes 1179664 | tf_op jit(solution)/shard_map/all_gather | solution.py:29
  266.7 2.5 convolution_convert_fusion.1
  269.3 40.1 %all-gather.13.cloned.1.call-done = bf16[768,768]{1,0:T(8,128)(2,1)} async-done(((bf16[96,768]{1,0:T(8,128)(2,1)}), bf16[768,768]{1,0:T(8,128)(2,1)}) %all-gather.13.cloned.1.call-update) | async-done | bytes 1179664 | tf_op jit(solution)/shard_map/all_gather | solution.py:29
  309.5 2.4 convolution_convert_fusion.3
  312.0 40.2 %all-gather.23.cloned.1.call-done = bf16[768,768]{1,0:T(8,128)(2,1)} async-done(((bf16[96,768]{1,0:T(8,128)(2,1)}), bf16[768,768]{1,0:T(8,128)(2,1)}) %all-gather.23.cloned.1.call-update) | async-done | bytes 1179664 | tf_op jit(solution)/shard_map/all_gather | solution.py:29
  352.2 2.9 fusion.33
  355.5 2.0 fusion.4
  357.9 2.0 fusion.6
  359.9 35.2 %all-gather.15.cloned.1.call-done = bf16[768,768]{1,0:T(8,128)(2,1)} async-done(((bf16[96,768]{1,0:T(8,128)(2,1)}), bf16[768,768]{1,0:T(8,128)(2,1)}) %all-gather.15.cloned.1.call-update) | async-done | bytes 1179664 | tf_op jit(solution)/shard_map/all_gather | solution.py:29
  395.1 2.5 fusion.31
  398.4 12.5 %all_to_all.27 = f32[8,96,12]{1,2,0:T(8,128)S(1)} all-to-all(f32[8,96,12]{1,2,0:T(8,128)S(1)} %copy.23), channel_id=1, replica_groups=mesh['dp'=64,'mp'=8] {'mp'}, dimensions={0} | all-to-all | bytes 73728 | tf_op jit(solution)/shard_map/all_to_all | solution.py:43
  411.6 28.3 %all_to_all.28 = f32[64,12,96]{2,1,0:T(8,128)S(1)} all-to-all(f32[64,12,96]{2,1,0:T(8,128)S(1)} %reshape.48), channel_id=1, replica_groups=mesh['dp'=64,'mp'=8] {'dp'}, dimensions={0} | all-to-all | bytes 589824 | tf_op jit(solution)/shard_map/all_to_all | solution.py:43
  440.6 17.9 %all_to_all.29 = bf16[64,12,96]{2,1,0:T(8,128)(2,1)S(1)} all-to-all(bf16[64,12,96]{2,1,0:T(8,128)(2,1)S(1)} %broadcast_in_dim.5), channel_id=1, replica_groups=mesh['dp'=64,'mp'=8] {'dp'}, dimensions={0} | all-to-all | bytes 294912 | tf_op jit(solution)/shard_map/all_to_all | solution.py:48
  459.4 3.1 fusion.26
  462.5 18.4 %all-gather.17.cloned.1.call-done = bf16[768,768]{1,0:T(8,128)(2,1)} async-done(((bf16[96,768]{1,0:T(8,128)(2,1)}), bf16[768,768]{1,0:T(8,128)(2,1)}) %all-gather.17.cloned.1.call-update) | async-done | bytes 1179664 | tf_op jit(solution)/shard_map/all_gather | solution.py:29
  480.9 3.1 fusion.28
  (86 shorter events, 7.0 us)
Async XLA Ops:
  7.2 92.6 %all-gather.27.cloned.1.call-start = ((), (), s32[]{:S(2)}) async-start(), calls=%async_computation.13 | async-start | bytes 1597440 | tf_op jit(solution)/shard_map/all_gather | solution.py:59
  8.6 153.4 %all-gather.11.cloned.1.call-start = ((), (), s32[]{:S(2)}) async-start(), calls=%async_computation.5 | async-start | bytes 5308416 | tf_op jit(solution)/shard_map/all_gather | solution.py:60
  9.9 31.5 %copy-start.20 = (f32[12,96]{1,0:T(8,128)S(1)}, f32[12,96]{1,0:T(8,128)}, u32[]{:S(2)}) copy-start(f32[12,96]{1,0:T(8,128)} %param.10) | copy-start | bytes 13828
  41.4 29.1 %copy-start.17 = (f32[12,96]{1,0:T(8,128)}, f32[12,96]{1,0:T(8,128)S(1)}, u32[]{:S(2)}) copy-start(f32[12,96]{1,0:T(8,128)S(1)} %get-tuple-element.31) | copy-start | bytes 13828
  70.6 1.2 copy-start.1
  71.7 133.4 %all-gather.19.cloned.1.call-start = ((), (), s32[]{:S(2)}) async-start(), calls=%async_computation.9 | async-start | bytes 1327104 | tf_op jit(solution)/shard_map/all_gather | solution.py:61
  72.5 194.2 %all-gather.21.cloned.1.call-start = ((), (), s32[]{:S(2)}) async-start(), calls=%async_computation.10 | async-start | bytes 1327104 | tf_op jit(solution)/shard_map/all_gather | solution.py:29
  171.3 1.0 copy-start.14
  172.3 1.6 copy-start.3
  173.8 4.2 copy-start.10
  173.8 1.8 copy-start.15
  178.1 47.4 %copy-start.11 = (f32[96,768]{1,0:T(8,128)}, f32[96,768]{1,0:T(8,128)S(1)}, u32[]{:S(2)}) copy-start(f32[96,768]{1,0:T(8,128)S(1)} %fusion.20) | copy-start | bytes 884740
  205.1 21.1 %copy-start.12 = (f32[96,768]{1,0:T(8,128)S(1)}, f32[96,768]{1,0:T(8,128)}, u32[]{:S(2)}) copy-start(f32[96,768]{1,0:T(8,128)} %get-tuple-element.33) | copy-start | bytes 884740
  225.5 84.0 %all-gather.13.cloned.1.call-start = ((), (), s32[]{:S(2)}) async-start(), calls=%async_computation.6 | async-start | bytes 1327104 | tf_op jit(solution)/shard_map/all_gather | solution.py:29
  226.9 82.6 %copy-start.4 = (bf16[96,768]{1,0:T(8,128)(2,1)S(1)}, bf16[96,768]{1,0:T(8,128)(2,1)}, u32[]{:S(2)}) copy-start(bf16[96,768]{1,0:T(8,128)(2,1)} %multiply_convert_fusion.1) | copy-start | bytes 442372
  226.9 125.3 %all-gather.23.cloned.1.call-start = ((), (), s32[]{:S(2)}) async-start(), calls=%async_computation.11 | async-start | bytes 1327104 | tf_op jit(solution)/shard_map/all_gather | solution.py:29
  269.2 83.0 %copy-start.5 = (bf16[96,768]{1,0:T(8,128)(2,1)S(1)}, bf16[96,768]{1,0:T(8,128)(2,1)}, u32[]{:S(2)}) copy-start(bf16[96,768]{1,0:T(8,128)(2,1)} %multiply_convert_fusion) | copy-start | bytes 442372
  269.3 83.0 %copy-start.9 = (bf16[96,768]{1,0:T(8,128)(2,1)S(1)}, bf16[96,768]{1,0:T(8,128)(2,1)}, u32[]{:S(2)}) copy-start(bf16[96,768]{1,0:T(8,128)(2,1)} %convolution_convert_fusion.1) | copy-start | bytes 442372
  269.3 125.9 %all-gather.15.cloned.1.call-start = ((), (), s32[]{:S(2)}) async-start(), calls=%async_computation.7 | async-start | bytes 1327104 | tf_op jit(solution)/shard_map/all_gather | solution.py:29
  311.9 43.5 %copy-start.13 = (f32[768,12]{0,1:T(8,128)S(1)}, f32[768,12]{0,1:T(8,128)}, u32[]{:S(2)}) copy-start(f32[768,12]{0,1:T(8,128)} %param.12) | copy-start | bytes 110596
  312.0 147.4 %all-gather.25.cloned.1.call-start = ((), (), s32[]{:S(2)}) async-start(), calls=%async_computation.12 | async-start | bytes 1327104 | tf_op jit(solution)/shard_map/all_gather | solution.py:29
  355.2 2.4 copy-start.18
  355.2 125.8 %all-gather.17.cloned.1.call-start = ((), (), s32[]{:S(2)}) async-start(), calls=%async_computation.8 | async-start | bytes 1327104 | tf_op jit(solution)/shard_map/all_gather | solution.py:29
  355.4 2.4 copy-start
  357.8 39.9 %copy-start.16 = (f32[12,96]{1,0:T(8,128)}, f32[12,96]{1,0:T(8,128)S(1)}, u32[]{:S(2)}) copy-start(f32[12,96]{1,0:T(8,128)S(1)} %fusion.47) | copy-start | bytes 13828
  357.9 37.3 %copy-start.2 = (bf16[768,768]{1,0:T(8,128)(2,1)S(1)}, bf16[768,768]{1,0:T(8,128)(2,1)}, u32[]{:S(2)}) copy-start(bf16[768,768]{1,0:T(8,128)(2,1)} %all-gather.13.cloned.1.call-done) | copy-start | bytes 3538948
  357.9 37.2 %copy-start.8 = (bf16[96,768]{1,0:T(8,128)(2,1)S(1)}, bf16[96,768]{1,0:T(8,128)(2,1)}, u32[]{:S(2)}) copy-start(bf16[96,768]{1,0:T(8,128)(2,1)} %convolution_convert_fusion.3) | copy-start | bytes 442372
  411.5 28.4 %copy-start.19 = (f32[12,96]{1,0:T(8,128)S(1)}, f32[12,96]{1,0:T(8,128)}, u32[]{:S(2)}) copy-start(f32[12,96]{1,0:T(8,128)} %param.9) | copy-start | bytes 13828
  439.8 19.5 %copy-start.6 = (bf16[96,768]{1,0:T(8,128)(2,1)S(1)}, bf16[96,768]{1,0:T(8,128)(2,1)}, u32[]{:S(2)}) copy-start(bf16[96,768]{1,0:T(8,128)(2,1)} %fusion.33) | copy-start | bytes 442372
  459.4 21.5 %copy-start.7 = (bf16[96,768]{1,0:T(8,128)(2,1)S(1)}, bf16[96,768]{1,0:T(8,128)(2,1)}, u32[]{:S(2)}) copy-start(bf16[96,768]{1,0:T(8,128)(2,1)} %fusion.31) | copy-start | bytes 442372
Sparse Core Ops, SparseCore 0:
  11.9 87.7 all-gather.26
  101.8 60.1 all-gather.10
  164.7 40.3 all-gather.18
  225.6 41.0 all-gather.20
  269.2 40.2 all-gather.12
  312.0 40.2 all-gather.22
  354.9 40.2 all-gather.14
  397.8 40.2 all-gather.24
  440.7 40.1 all-gather.16
where the time goes:
time: 491 us
  waiting for transfers between devices  287 us (58%)
  blocking collectives  135 us (27%)
  matrix products  30.2 us (6%)
  local copies, waits for them, and re-layouts  16.3 us (3%)
  between operations  15.6 us (3%)
  other arithmetic  5.29 us (1%)
    all_gather x6, waiting for transfers between devices, all_rows(): lax.all_gather(for_sending(pair), 'mp', axis=0, tiled=True)  174 us
    all_to_all x3, blocking collectives, scatter_sum(): return jnp.sum(lax.all_to_all(chunks, axis, 0, 0, tiled=False), axis=0)  72.1 us
    all_gather x1, waiting for transfers between devices, per_device(): both_full = lax.all_gather(pieces, 'mp', axis=2, tiled=True)  59.1 us
    all_to_all x2, blocking collectives, gather_rows(): lax.all_to_all(jnp.broadcast_to(x[None], (count,) + x.shape), axis, 0, 0,...  46.8 us
    all_gather x1, waiting for transfers between devices, per_device(): right_full = lax.all_gather(right_basis, 'mp', axis=1, tiled=True)  27 us
    all_gather x1, waiting for transfers between devices, per_device(): left_full = lax.all_gather(left_basis, 'dp', axis=1, tiled=True)  27 us
    psum x1, blocking collectives, per_device(): lax.psum((jnp.sum(power_left * power_left), jnp.sum(power_right * power_r...  16.5 us
  transfers between devices with their start and end apart: 9, of which 8 were waited for; matrix products, arithmetic and copies ran while one was open for 9% of the time, Pallas kernels for 0%

commit v1 on v0

--- a/solution.py
+++ b/solution.py
@@ -1,3 +1,4 @@
+import functools
 import jax
 import jax.numpy as jnp
 from jax import lax
@@ -15,6 +16,33 @@
 highest = lax.Precision.HIGHEST
 
 
+def see_array(original, a_name, d_out):
+    r1 = lax.axis_size(a_name)
+    local_out, f_now, w1 = (r1, lax.axis_index(a_name), original.shape[d_out])
+    seen = [(pp, (pp + 1) % local_out) for pp in range(local_out)]
+    sheets = [(pp, (pp - 1) % local_out) for pp in range(local_out)]
+    kept_arr = jnp.zeros(
+        (*original.shape[:d_out], local_out * w1, *original.shape[d_out + 1 :]), original.dtype
+    )
+    kept_arr = lax.dynamic_update_slice_in_dim(kept_arr, original, f_now * w1, axis=d_out)
+    piece_now = big = original
+    placed = local_out // 2
+    for num in range(1, placed + 1):
+        piece_now = lax.ppermute(piece_now, a_name, seen)
+        kept_arr = lax.dynamic_update_slice_in_dim(
+            kept_arr, piece_now, (f_now - num) % local_out * w1, axis=d_out
+        )
+        if num < local_out - placed:
+            big = lax.ppermute(big, a_name, sheets)
+            kept_arr = lax.dynamic_update_slice_in_dim(
+                kept_arr, big, (f_now + num) % local_out * w1, axis=d_out
+            )
+    return kept_arr
+
+
+take_wires = functools.partial(see_array, a_name="mp", d_out=1)
+
+
 def for_sending(x):
 
     def short(part):
@@ -58,7 +86,7 @@
     pieces = jnp.swapaxes(pieces, 0, 1).reshape(2, -1, pieces.shape[-1])
     left_full = lax.all_gather(left_basis, "dp", axis=1, tiled=True)
     both_full = lax.all_gather(pieces, "mp", axis=2, tiled=True)
-    right_full = lax.all_gather(right_basis, "mp", axis=1, tiled=True)
+    right_full = take_wires(right_basis)
     grad_full = both_full[0]
     moment_full = both_full[1]
 

time: 491 us -> 464 us (0.945)
  waiting for transfers between devices: 287 us -> 234 us
  starting transfers between devices: 0.77 us -> 24 us
    all_gather x1 -> x0, waiting for transfers between devices: 27 us -> none  [per_device(): right_full = lax.all_gather(right_basis, 'mp', axis=1, tiled=True)]
    all_gather x1, waiting for transfers between devices: 27 us -> 0.02 us  [per_device(): left_full = lax.all_gather(left_basis, 'dp', axis=1, tiled=True)]
    ppermute x0 -> x7, starting transfers between devices: none -> 23.4 us  [the longest x3 14.1 us: see_array(): big = lax.ppermute(big, a_name, sheets)]
    ppermute x0 -> x7, waiting for transfers between devices: none -> 9.66 us  [the longest x4 9.66 us: see_array(): piece_now = lax.ppermute(piece_now, a_name, seen)]
    all_gather x1, waiting for transfers between devices: 59.1 us -> 52.7 us  [per_device(): both_full = lax.all_gather(pieces, 'mp', axis=2, tiled=True)]
  transfers between devices with their start and end apart: 9 -> 15, of which waited for: 8 -> 10; matrix products, arithmetic and copies ran while one was open for 9% -> 6% of each run, Pallas kernels for 0% -> 0%
where the time goes in v1:
time: 464 us; the launch traced here: 463 us
  waiting for transfers between devices  234 us (50%)
  blocking collectives  135 us (29%)
  matrix products  30.4 us (7%)
  starting transfers between devices  24 us (5%)
  local copies, waits for them, and re-layouts  17.3 us (4%)
  between operations  16.1 us (3%)
  other arithmetic  6.54 us (1%)
    all_gather x6, waiting for transfers between devices, all_rows(): lax.all_gather(for_sending(pair), 'mp', axis=0, tiled=True)  171 us
    all_to_all x3, blocking collectives, scatter_sum(): return jnp.sum(lax.all_to_all(chunks, axis, 0, 0, tiled=False), axis=0)  72.1 us
    all_gather x1, waiting for transfers between devices, per_device(): both_full = lax.all_gather(pieces, 'mp', axis=2, tiled=True)  52.7 us
    all_to_all x2, blocking collectives, gather_rows(): lax.all_to_all(jnp.broadcast_to(x[None], (count,) + x.shape), axis, 0, 0,...  46.8 us
    psum x1, blocking collectives, per_device(): lax.psum((jnp.sum(power_left * power_left), jnp.sum(power_right * power_r...  16.2 us
    ppermute x3, starting transfers between devices, see_array(): big = lax.ppermute(big, a_name, sheets)  14.1 us
    ppermute x4, waiting for transfers between devices, see_array(): piece_now = lax.ppermute(piece_now, a_name, seen)  9.66 us
    ppermute x4, starting transfers between devices, see_array(): piece_now = lax.ppermute(piece_now, a_name, seen)  9.38 us
  transfers between devices with their start and end apart: 15, of which 10 were waited for; matrix products, arithmetic and copies ran while one was open for 6% of the time, Pallas kernels for 0%

profile of v1, /device:TPU:2, one launch (start us, length us, event | category | flops | bytes accessed | tf_op | source)
XLA Modules:
  0.0 463.1 jit_solution(7791195882344587852)
XLA Ops:
  10.0 31.4 %all_to_all.25 = f32[64,12,96]{2,1,0:T(8,128)S(1)} all-to-all(f32[64,12,96]{2,1,0:T(8,128)S(1)} %reshape.45), channel_id=1, replica_groups=mesh['dp'=64,'mp'=8] {'dp'}, dimensions={0} | all-to-all | bytes 589824 | tf_op jit(solution)/shard_map/all_to_all | solution.py:71
  41.7 28.9 %all_to_all.26 = f32[64,2,12,96]{3,1,2,0:T(2,128)S(1)} all-to-all(f32[64,2,12,96]{3,1,2,0:T(2,128)S(1)} %broadcast_in_dim.6), channel_id=1, replica_groups=mesh['dp'=64,'mp'=8] {'dp'}, dimensions={0} | all-to-all | bytes 1179648 | tf_op jit(solution)/shard_map/all_to_all | solution.py:76
  72.7 3.5 collective-permute-start
  76.1 3.8 collective-permute-start.1
  81.4 1.9 collective-permute-start.2
  83.3 5.1 %collective-permute-start.3 = (bf16[768,96]{0,1:T(8,128)(2,1)S(1)}, bf16[768,96]{0,1:T(8,128)(2,1)S(1)}, u32[]{:S(2)}, u32[]{:S(2)}) collective-permute-start(bf16[768,96]{0,1:T(8,128)(2,1)S(1)} %collective-permute-done.1), channel_id=1, source_target_pairs={{0,7},{1,0},{2,1},{3,2},{4,3},{5,4},{6,5},{7,6},{8,15},{9,8},{10,9... | collective-permute-start | bytes 442376 | tf_op jit(solution)/shard_map/ppermute | solution.py:36
  89.7 1.9 collective-permute-start.4
  91.6 5.1 %collective-permute-start.5 = (bf16[768,96]{0,1:T(8,128)(2,1)S(1)}, bf16[768,96]{0,1:T(8,128)(2,1)S(1)}, u32[]{:S(2)}, u32[]{:S(2)}) collective-permute-start(bf16[768,96]{0,1:T(8,128)(2,1)S(1)} %collective-permute-done.3), channel_id=1, source_target_pairs={{0,7},{1,0},{2,1},{3,2},{4,3},{5,4},{6,5},{7,6},{8,15},{9,8},{10,9... | collective-permute-start | bytes 442376 | tf_op jit(solution)/shard_map/ppermute | solution.py:36
  97.9 2.1 collective-permute-start.6
  100.0 6.1 %collective-permute-done.6 = bf16[768,96]{0,1:T(8,128)(2,1)S(1)} collective-permute-done((bf16[768,96]{0,1:T(8,128)(2,1)S(1)}, bf16[768,96]{0,1:T(8,128)(2,1)S(1)}, u32[]{:S(2)}, u32[]{:S(2)}) %collective-permute-start.6) | collective-permute-done | bytes 147488 | tf_op jit(solution)/shard_map/ppermute | solution.py:31
  106.2 3.1 reshape.52
  109.3 52.7 %all-gather.10.cloned.1.call-done = f32[2,768,768]{1,0,2:T(2,128)} async-done(((f32[2,768,96]{1,0,2:T(2,128)}), f32[2,768,768]{1,0,2:T(2,128)}) %all-gather.10.cloned.1.call-update) | async-done | bytes 4718608 | tf_op jit(solution)/shard_map/all_gather | solution.py:88
  162.0 9.3 %fusion.53 = (f32[1,768,768]{1,0,2:T(1,128)S(1)}, f32[1,768,768]{1,0,2:T(1,128)}) fusion(f32[2,768,768]{1,0,2:T(2,128)} %all-gather.10.cloned.1.call-done), kind=kLoop, calls=%fused_computation.78 | loop fusion | bytes 9437184 | tf_op jit(solution)/shard_map/slice | solution.py:90
  173.8 2.4 fusion.20
  176.3 1.8 multiply_reduce_fusion.1
  179.9 16.2 %all-reduce = (f32[]{:T(128)}, f32[]{:T(128)}) all-reduce(f32[]{:T(128)} %get-tuple-element.35, f32[]{:T(128)} %get-tuple-element.37), channel_id=1, replica_groups=mesh['dp'=64,'mp'=8] {'mp'}, use_global_device_ids=true, to_apply=%region_5.6 | all-reduce | flops 2 | bytes 16 | tf_op jit(solution)/shard_map/psum | solution.py:132
  200.9 39.3 %all-gather.12.cloned.1.call-done = bf16[768,768]{1,0:T(8,128)(2,1)} async-done(((bf16[96,768]{1,0:T(8,128)(2,1)}), bf16[768,768]{1,0:T(8,128)(2,1)}) %all-gather.12.cloned.1.call-update) | async-done | bytes 1179664 | tf_op jit(solution)/shard_map/all_gather | solution.py:57
  240.2 2.5 convolution_convert_fusion.3
  242.8 39.6 %all-gather.18.cloned.1.call-done = bf16[768,768]{1,0:T(8,128)(2,1)} async-done(((bf16[96,768]{1,0:T(8,128)(2,1)}), bf16[768,768]{1,0:T(8,128)(2,1)}) %all-gather.18.cloned.1.call-update) | async-done | bytes 1179664 | tf_op jit(solution)/shard_map/all_gather | solution.py:57
  282.4 2.5 convolution_convert_fusion.1
  285.0 40.2 %all-gather.14.cloned.1.call-done = bf16[768,768]{1,0:T(8,128)(2,1)} async-done(((bf16[96,768]{1,0:T(8,128)(2,1)}), bf16[768,768]{1,0:T(8,128)(2,1)}) %all-gather.14.cloned.1.call-update) | async-done | bytes 1179664 | tf_op jit(solution)/shard_map/all_gather | solution.py:57
  325.2 2.6 fusion.31
  328.1 3.0 fusion.4
  331.5 2.0 fusion.6
  333.6 33.8 %all-gather.20.cloned.1.call-done = bf16[768,768]{1,0:T(8,128)(2,1)} async-done(((bf16[96,768]{1,0:T(8,128)(2,1)}), bf16[768,768]{1,0:T(8,128)(2,1)}) %all-gather.20.cloned.1.call-update) | async-done | bytes 1179664 | tf_op jit(solution)/shard_map/all_gather | solution.py:57
  367.3 2.5 fusion.33
  370.6 12.5 %all_to_all.27 = f32[8,96,12]{1,2,0:T(8,128)S(1)} all-to-all(f32[8,96,12]{1,2,0:T(8,128)S(1)} %copy.23), channel_id=1, replica_groups=mesh['dp'=64,'mp'=8] {'mp'}, dimensions={0} | all-to-all | bytes 73728 | tf_op jit(solution)/shard_map/all_to_all | solution.py:71
  383.8 28.3 %all_to_all.28 = f32[64,12,96]{2,1,0:T(8,128)S(1)} all-to-all(f32[64,12,96]{2,1,0:T(8,128)S(1)} %reshape.48), channel_id=1, replica_groups=mesh['dp'=64,'mp'=8] {'dp'}, dimensions={0} | all-to-all | bytes 589824 | tf_op jit(solution)/shard_map/all_to_all | solution.py:71
  412.8 17.9 %all_to_all.29 = bf16[64,12,96]{2,1,0:T(8,128)(2,1)S(1)} all-to-all(bf16[64,12,96]{2,1,0:T(8,128)(2,1)S(1)} %broadcast_in_dim.7), channel_id=1, replica_groups=mesh['dp'=64,'mp'=8] {'dp'}, dimensions={0} | all-to-all | bytes 294912 | tf_op jit(solution)/shard_map/all_to_all | solution.py:76
  431.6 3.1 fusion.28
  434.7 18.4 %all-gather.22.cloned.1.call-done = bf16[768,768]{1,0:T(8,128)(2,1)} async-done(((bf16[96,768]{1,0:T(8,128)(2,1)}), bf16[768,768]{1,0:T(8,128)(2,1)}) %all-gather.22.cloned.1.call-update) | async-done | bytes 1179664 | tf_op jit(solution)/shard_map/all_gather | solution.py:57
  453.1 3.1 fusion.26
  (105 shorter events, 20.4 us)
Async XLA Ops:
  7.2 99.0 %all-gather.24.cloned.1.call-start = ((), (), s32[]{:S(2)}) async-start(), calls=%async_computation.12 | async-start | bytes 1597440 | tf_op jit(solution)/shard_map/all_gather | solution.py:87
  8.6 153.4 %all-gather.10.cloned.1.call-start = ((), (), s32[]{:S(2)}) async-start(), calls=%async_computation.5 | async-start | bytes 5308416 | tf_op jit(solution)/shard_map/all_gather | solution.py:88
  9.9 31.5 %copy-start.20 = (f32[12,96]{1,0:T(8,128)S(1)}, f32[12,96]{1,0:T(8,128)}, u32[]{:S(2)}) copy-start(f32[12,96]{1,0:T(8,128)} %param.10) | copy-start | bytes 13828
  41.4 29.1 %copy-start.17 = (f32[12,96]{1,0:T(8,128)}, f32[12,96]{1,0:T(8,128)S(1)}, u32[]{:S(2)}) copy-start(f32[12,96]{1,0:T(8,128)S(1)} %get-tuple-element.34) | copy-start | bytes 13828
  71.7 168.5 %all-gather.12.cloned.1.call-start = ((), (), s32[]{:S(2)}) async-start(), calls=%async_computation.6 | async-start | bytes 1327104 | tf_op jit(solution)/shard_map/all_gather | solution.py:57
  72.7 8.8 %collective-permute-start = (bf16[768,96]{0,1:T(8,128)(2,1)S(1)}, bf16[768,96]{0,1:T(8,128)(2,1)S(1)}, u32[]{:S(2)}, u32[]{:S(2)}) collective-permute-start(bf16[768,96]{0,1:T(8,128)(2,1)S(1)} %get-tuple-element.30), channel_id=1, source_target_pairs={{0,1},{1,2},{2,3},{3,4},{4,5},{5,6},{6,7},{7,0},{8,9},{9,10},{10,1... | collective-permute-start | bytes 442376 | tf_op jit(solution)/shard_map/ppermute | solution.py:31
  76.1 7.2 %collective-permute-start.1 = (bf16[768,96]{0,1:T(8,128)(2,1)S(1)}, bf16[768,96]{0,1:T(8,128)(2,1)S(1)}, u32[]{:S(2)}, u32[]{:S(2)}) collective-permute-start(bf16[768,96]{0,1:T(8,128)(2,1)S(1)} %get-tuple-element.30), channel_id=1, source_target_pairs={{0,7},{1,0},{2,1},{3,2},{4,3},{5,4},{6,5},{7,6},{8,15},{9,8},{10,9... | collective-permute-start | bytes 442376 | tf_op jit(solution)/shard_map/ppermute | solution.py:36
  81.4 8.2 %collective-permute-start.2 = (bf16[768,96]{0,1:T(8,128)(2,1)S(1)}, bf16[768,96]{0,1:T(8,128)(2,1)S(1)}, u32[]{:S(2)}, u32[]{:S(2)}) collective-permute-start(bf16[768,96]{0,1:T(8,128)(2,1)S(1)} %collective-permute-done), channel_id=1, source_target_pairs={{0,1},{1,2},{2,3},{3,4},{4,5},{5,6},{6,7},{7,0},{8,9},{9,10},{10,1... | collective-permute-start | bytes 442376 | tf_op jit(solution)/shard_map/ppermute | solution.py:31
  83.3 8.2 %collective-permute-start.3 = (bf16[768,96]{0,1:T(8,128)(2,1)S(1)}, bf16[768,96]{0,1:T(8,128)(2,1)S(1)}, u32[]{:S(2)}, u32[]{:S(2)}) collective-permute-start(bf16[768,96]{0,1:T(8,128)(2,1)S(1)} %collective-permute-done.1), channel_id=1, source_target_pairs={{0,7},{1,0},{2,1},{3,2},{4,3},{5,4},{6,5},{7,6},{8,15},{9,8},{10,9... | collective-permute-start | bytes 442376 | tf_op jit(solution)/shard_map/ppermute | solution.py:36
  89.7 8.2 %collective-permute-start.4 = (bf16[768,96]{0,1:T(8,128)(2,1)S(1)}, bf16[768,96]{0,1:T(8,128)(2,1)S(1)}, u32[]{:S(2)}, u32[]{:S(2)}) collective-permute-start(bf16[768,96]{0,1:T(8,128)(2,1)S(1)} %collective-permute-done.2), channel_id=1, source_target_pairs={{0,1},{1,2},{2,3},{3,4},{4,5},{5,6},{6,7},{7,0},{8,9},{9,10},{10,1... | collective-permute-start | bytes 442376 | tf_op jit(solution)/shard_map/ppermute | solution.py:31
  91.6 8.4 %collective-permute-start.5 = (bf16[768,96]{0,1:T(8,128)(2,1)S(1)}, bf16[768,96]{0,1:T(8,128)(2,1)S(1)}, u32[]{:S(2)}, u32[]{:S(2)}) collective-permute-start(bf16[768,96]{0,1:T(8,128)(2,1)S(1)} %collective-permute-done.3), channel_id=1, source_target_pairs={{0,7},{1,0},{2,1},{3,2},{4,3},{5,4},{6,5},{7,6},{8,15},{9,8},{10,9... | collective-permute-start | bytes 442376 | tf_op jit(solution)/shard_map/ppermute | solution.py:36
  97.9 8.2 %collective-permute-start.6 = (bf16[768,96]{0,1:T(8,128)(2,1)S(1)}, bf16[768,96]{0,1:T(8,128)(2,1)S(1)}, u32[]{:S(2)}, u32[]{:S(2)}) collective-permute-start(bf16[768,96]{0,1:T(8,128)(2,1)S(1)} %collective-permute-done.4), channel_id=1, source_target_pairs={{0,1},{1,2},{2,3},{3,4},{4,5},{5,6},{6,7},{7,0},{8,9},{9,10},{10,1... | collective-permute-start | bytes 442376 | tf_op jit(solution)/shard_map/ppermute | solution.py:31
  173.8 2.4 copy-start.10
  176.3 3.6 copy-start.11
  198.5 83.9 %all-gather.18.cloned.1.call-start = ((), (), s32[]{:S(2)}) async-start(), calls=%async_computation.9 | async-start | bytes 1327104 | tf_op jit(solution)/shard_map/all_gather | solution.py:57
  200.9 124.3 %all-gather.14.cloned.1.call-start = ((), (), s32[]{:S(2)}) async-start(), calls=%async_computation.7 | async-start | bytes 1327104 | tf_op jit(solution)/shard_map/all_gather | solution.py:57
  242.7 82.4 %copy-start.4 = (bf16[768,768]{1,0:T(8,128)(2,1)S(1)}, bf16[768,768]{1,0:T(8,128)(2,1)}, u32[]{:S(2)}) copy-start(bf16[768,768]{1,0:T(8,128)(2,1)} %all-gather.12.cloned.1.call-done) | copy-start | bytes 3538948
  242.8 124.6 %all-gather.20.cloned.1.call-start = ((), (), s32[]{:S(2)}) async-start(), calls=%async_computation.10 | async-start | bytes 1327104 | tf_op jit(solution)/shard_map/all_gather | solution.py:57
  284.9 146.7 %all-gather.16.cloned.1.call-start = ((), (), s32[]{:S(2)}) async-start(), calls=%async_computation.8 | async-start | bytes 1327104 | tf_op jit(solution)/shard_map/all_gather | solution.py:57
  327.8 3.3 copy-start.2
  327.8 3.3 copy-start.18
  327.8 125.3 %all-gather.22.cloned.1.call-start = ((), (), s32[]{:S(2)}) async-start(), calls=%async_computation.11 | async-start | bytes 1327104 | tf_op jit(solution)/shard_map/all_gather | solution.py:57
  328.1 3.4 copy-start
  328.1 3.4 copy-start.12
  331.4 38.5 %copy-start.16 = (f32[12,96]{1,0:T(8,128)}, f32[12,96]{1,0:T(8,128)S(1)}, u32[]{:S(2)}) copy-start(f32[12,96]{1,0:T(8,128)S(1)} %fusion.47) | copy-start | bytes 13828
  331.5 35.8 %copy-start.3 = (bf16[768,768]{1,0:T(8,128)(2,1)S(1)}, bf16[768,768]{1,0:T(8,128)(2,1)}, u32[]{:S(2)}) copy-start(bf16[768,768]{1,0:T(8,128)(2,1)} %all-gather.18.cloned.1.call-done) | copy-start | bytes 3538948
  331.5 35.8 %copy-start.6 = (bf16[96,768]{1,0:T(8,128)(2,1)S(1)}, bf16[96,768]{1,0:T(8,128)(2,1)}, u32[]{:S(2)}) copy-start(bf16[96,768]{1,0:T(8,128)(2,1)} %multiply_convert_fusion) | copy-start | bytes 442372
  331.5 35.8 %copy-start.9 = (bf16[96,768]{1,0:T(8,128)(2,1)S(1)}, bf16[96,768]{1,0:T(8,128)(2,1)}, u32[]{:S(2)}) copy-start(bf16[96,768]{1,0:T(8,128)(2,1)} %convolution_convert_fusion.1) | copy-start | bytes 442372
  369.9 13.2 %copy-start.13 = (f32[768,12]{0,1:T(8,128)S(1)}, f32[768,12]{0,1:T(8,128)}, u32[]{:S(2)}) copy-start(f32[768,12]{0,1:T(8,128)} %param.12) | copy-start | bytes 110596
  383.7 28.4 %copy-start.19 = (f32[12,96]{1,0:T(8,128)S(1)}, f32[12,96]{1,0:T(8,128)}, u32[]{:S(2)}) copy-start(f32[12,96]{1,0:T(8,128)} %param.9) | copy-start | bytes 13828
  412.1 19.5 %copy-start.7 = (bf16[96,768]{1,0:T(8,128)(2,1)S(1)}, bf16[96,768]{1,0:T(8,128)(2,1)}, u32[]{:S(2)}) copy-start(bf16[96,768]{1,0:T(8,128)(2,1)} %fusion.31) | copy-start | bytes 442372
  431.6 21.5 %copy-start.8 = (bf16[96,768]{1,0:T(8,128)(2,1)S(1)}, bf16[96,768]{1,0:T(8,128)(2,1)}, u32[]{:S(2)}) copy-start(bf16[96,768]{1,0:T(8,128)(2,1)} %fusion.33) | copy-start | bytes 442372
  (4 other events, 5.9 us)
Sparse Core Ops, SparseCore 0:
  11.9 87.7 all-gather.23
  101.8 60.2 all-gather.9
  198.6 41.5 all-gather.11
  242.2 40.2 all-gather.17
  284.9 40.2 all-gather.13
  327.1 40.2 all-gather.19
  370.0 40.2 all-gather.15
  412.9 40.1 all-gather.21
